TPU v7x, 256 devices: a whole 4x4x8 slice. The times are simulated.
256 devices in a mesh: member: 4 (over z_hi), token: 64 (over z_lo, x, y, core).
Axes of the slice: x: 4, y: 4, z: 8 (z_hi: 4, z_lo: 2; z = z_hi * 2 + z_lo), core: 2. Of those that a mesh axis runs over, the one named last changes fastest.
Arguments:
- members_in: bfloat16 [8, 8192, 1024], P('member', 'token'), may hold values from -16 to 16
- member_noise: bfloat16 [8, 8192, 1024], P('member', 'token'), may hold values from -6 to 6
- norm_gain: float32 [1024], replicated, may hold values from 0.25 to 1.75
- weight_query: bfloat16 [1024, 1024], replicated, may hold values from -0.1875 to 0.1875
- weight_key: bfloat16 [1024, 1024], replicated, may hold values from -0.1875 to 0.1875
- weight_value: bfloat16 [1024, 1024], replicated, may hold values from -0.1875 to 0.1875
- weight_out: bfloat16 [1024, 1024], replicated, may hold values from -0.1875 to 0.1875
- decoder_projection_weight: bfloat16 [100, 1024], replicated, may hold values from -0.1875 to 0.1875
- decoder_bias: float32 [100], replicated, may hold values from -3 to 3
- observations: float32 [100, 65536], P(None, 'token'), may hold values from -6 to 6
- surface_extent_factor: float32 [65536], P('token'), may hold values from 0.3 to 3
- quantity_scoring_factor: float32 [100], replicated, may hold values from 0.2 to 2
- point_map: int32 [65536], P('token'), may hold values from 0 to 127
Outputs:
- mean_scoring: float32 [], replicated
- grad_members: bfloat16 [8, 8192, 1024], P('member', 'token')
- grad_out: float32 [1024, 1024], P('token')
- grad_decoder: float32 [100, 1024], replicated
Inputs may be any that keep to these rules, and one draw needn't show every extreme that they name: Point p belongs to token (p // 1024) * 128 + point_map[p].
All inputs are finite; a program needn't handle non-finite values.
Results may differ from a plain program's by a relative error of at most 0.015.
Values may be sent and summed in bfloat16 or wider, within the bound.
No kernel may reach another device: no remote copies, remote signals or barrier semaphores. Data moves between devices by JAX's collectives and lax.ppermute only.
A program may use at most 128 MiB of HBM per device.

v0:
```python
import jax
import jax.numpy as jnp
from jax import lax
from jax.sharding import PartitionSpec as P

HEADS = 16
HALF = 128
EPSILON = 1e-06
SMOOTH = 0.01


def extended_2(block, sides, width):
    for axis, dim in sides:
        count = lax.axis_size(axis)
        forward = [(i, i + 1) for i in range(count - 1)]
        backward = [(target, source) for source, target in forward]
        low = lax.ppermute(
            lax.slice_in_dim(block, block.shape[dim] - width, None, axis=dim), axis, forward
        )
        high = lax.ppermute(lax.slice_in_dim(block, 0, width, axis=dim), axis, backward)
        block = jnp.concatenate([low, block, high], axis=dim)
    return block


def from_behind(block, axis, distance):
    devices = range(lax.axis_size(axis))
    route = [(i - distance, i) for i in devices if i - distance in devices]
    return lax.ppermute(block, axis, route)


def normalize_heads(flat):
    rows, width = flat.shape
    split = flat.reshape(rows, HEADS, width // HEADS)
    split = split * lax.rsqrt(jnp.mean(split * split, axis=-1, keepdims=True) + EPSILON)
    return split.reshape(rows, width)


def project(state_in, member_noise, norm_gain, weight_query, weight_key, weight_value):
    member_rows, tokens, width = state_in.shape
    mixed = state_in + member_noise.astype(jnp.float32)
    normed = (
        mixed * lax.rsqrt(jnp.mean(mixed * mixed, axis=-1, keepdims=True) + EPSILON) * norm_gain
    ).astype(jnp.bfloat16)
    flat = normed.reshape(member_rows * tokens, width)
    query = normalize_heads(jnp.dot(flat, weight_query, preferred_element_type=jnp.float32)).astype(
        jnp.bfloat16
    )
    key = normalize_heads(jnp.dot(flat, weight_key, preferred_element_type=jnp.float32)).astype(
        jnp.bfloat16
    )
    value = jnp.dot(flat, weight_value, preferred_element_type=jnp.float32).astype(jnp.bfloat16)
    full_shape = (member_rows, tokens, width)
    return (query.reshape(full_shape), key.reshape(full_shape), value.reshape(full_shape))


def attend(query, keys, values, leading_realization, total):
    member_rows, queries, width = query.shape
    realization_number = keys.shape[1]
    depth = width // HEADS
    query_heads = query.reshape(member_rows, queries, HEADS, depth)
    key_heads = keys.reshape(member_rows, realization_number, HEADS, depth)
    value_heads = values.reshape(member_rows, realization_number, HEADS, depth)
    scores = jnp.einsum(
        "mqhd,mkhd->mhqk", query_heads, key_heads, preferred_element_type=jnp.float32
    ) / jnp.sqrt(jnp.float32(depth))
    query_pos = leading_realization + lax.iota(jnp.int32, queries)
    key_pos = leading_realization - HALF + lax.iota(jnp.int32, realization_number)
    allowed = (key_pos[None, :] >= query_pos[:, None] - HALF) & (
        key_pos[None, :] < query_pos[:, None] + HALF
    )
    allowed = allowed & (key_pos[None, :] >= 0) & (key_pos[None, :] < total)
    raised = jnp.where(allowed[None, None], jnp.exp(scores), jnp.float32(0.0))
    probs = (raised / jnp.sum(raised, axis=-1, keepdims=True)).astype(jnp.bfloat16)
    mixed = jnp.einsum("mhqk,mkhd->mqhd", probs, value_heads, preferred_element_type=jnp.float32)
    return mixed.reshape(member_rows, queries, width).astype(jnp.bfloat16)


def softened_magnitude(diff):
    return jnp.sqrt(diff * diff + SMOOTH)


def unbiased_ranked_score(
    realization_prediction, observed_grid, surface_extent, quantity_scoring_factor
):
    realization_number = realization_prediction.shape[0]
    accuracy_part = softened_magnitude(realization_prediction[0] - observed_grid)
    for realization_position in range(1, realization_number):
        accuracy_part = accuracy_part + softened_magnitude(
            realization_prediction[realization_position] - observed_grid
        )
    dispersion_part = jnp.zeros_like(accuracy_part)
    for leading_realization in range(realization_number):
        for paired_realization in range(leading_realization + 1, realization_number):
            dispersion_part = dispersion_part + softened_magnitude(
                realization_prediction[leading_realization]
                - realization_prediction[paired_realization]
            )
    score = accuracy_part / realization_number - dispersion_part / (
        realization_number * (realization_number - 1)
    )
    return jnp.sum(quantity_scoring_factor[:, None] * surface_extent[None, :] * score)


def shards(
    members_in,
    member_noise,
    norm_gain,
    weight_query,
    weight_key,
    weight_value,
    weight_out,
    decoder_projection_weight,
    decoder_bias,
    observations,
    surface_extent_factor,
    quantity_scoring_factor,
    point_map,
):
    member_rows, tokens, width = members_in.shape
    state = members_in.astype(jnp.float32)

    def front(state_in):
        return project(state_in, member_noise, norm_gain, weight_query, weight_key, weight_value)

    (query, key, value), front_pull = jax.vjp(front, state)
    stacked = jnp.stack([key, value])
    extended = extended_2(stacked, (("token", 2),), HALF)
    leading_realization = lax.axis_index("token") * tokens
    total = tokens * lax.axis_size("token")

    def middle(query_in, extended_in):
        return attend(query_in, extended_in[0], extended_in[1], leading_realization, total)

    attended, middle_pull = jax.vjp(middle, query, extended)
    flat_att = attended.reshape(member_rows * tokens, width)
    update = jnp.dot(flat_att, weight_out, preferred_element_type=jnp.float32).reshape(
        member_rows, tokens, width
    )
    residual_stream_state = (state + member_noise.astype(jnp.float32) + update).astype(jnp.bfloat16)

    def decode_tokens(residual_in, decoder_in):
        mapping_array = jnp.einsum(
            "vc,mtc->mvt",
            decoder_in.astype(jnp.bfloat16),
            residual_in,
            preferred_element_type=jnp.float32,
        )
        mapping_array = mapping_array + decoder_bias[None, :, None]
        return jnp.take(mapping_array, point_map, axis=2)

    realization_prediction, readout_slope_pulled = jax.vjp(
        decode_tokens, residual_stream_state, decoder_projection_weight.astype(jnp.float32)
    )
    location_places = realization_prediction.shape[2]
    groups = lax.axis_size("member")
    local_shard = lax.axis_index("member")
    gathered_lines = lax.all_gather(realization_prediction, "member", axis=0, tiled=True)

    def score_all(whole):
        return unbiased_ranked_score(
            whole, observations, surface_extent_factor, quantity_scoring_factor
        )

    full_loss, score_pull = jax.vjp(score_all, gathered_lines)
    (complete_gradient,) = score_pull(jnp.ones((), jnp.float32))
    prediction_slope = lax.dynamic_slice_in_dim(
        complete_gradient, local_shard * member_rows, member_rows, 0
    )
    partial_loss = full_loss / groups
    carried_slope, readout_piece_result = readout_slope_pulled(prediction_slope)
    overall_scoring_amount, grad_decoder = lax.psum(
        (partial_loss, readout_piece_result), ("member", "token")
    )
    mean_scoring = overall_scoring_amount / (
        realization_prediction.shape[1] * location_places * lax.axis_size("token")
    )
    flat_grad = carried_slope.reshape(member_rows * tokens, width)
    grad_attended = (
        jnp.dot(flat_grad, weight_out.T, preferred_element_type=jnp.float32)
        .astype(jnp.bfloat16)
        .reshape(member_rows, tokens, width)
    )
    grad_query, grad_extended = middle_pull(grad_attended)
    lower_rim = grad_extended[:, :, :HALF]
    upper_rim = grad_extended[:, :, tokens + HALF :]
    inner = grad_extended[:, :, HALF : tokens + HALF].astype(jnp.float32)
    from_next = from_behind(lower_rim, "token", -1)
    from_prev = from_behind(upper_rim, "token", 1)
    inner = inner.at[:, :, tokens - HALF :].add(from_next.astype(jnp.float32))
    inner = inner.at[:, :, :HALF].add(from_prev.astype(jnp.float32))
    (grad_front,) = front_pull(
        (grad_query, inner[0].astype(jnp.bfloat16), inner[1].astype(jnp.bfloat16))
    )
    grad_members = (grad_front + carried_slope.astype(jnp.float32)).astype(jnp.bfloat16)
    contract = (((0,), (0,)), ((), ()))
    product = lax.dot_general(flat_att, flat_grad, contract, preferred_element_type=jnp.float32)
    summed = lax.psum(product.astype(jnp.bfloat16), "member").astype(jnp.float32)
    grad_out = lax.psum_scatter(summed, "token", scatter_dimension=0, tiled=True)
    return (mean_scoring, grad_members, grad_out, grad_decoder)


def solution(mesh):
    return jax.shard_map(
        shards,
        mesh=mesh,
        in_specs=(
            P("member", "token", None),
            P("member", "token", None),
            P(),
            P(),
            P(),
            P(),
            P(),
            P(),
            P(),
            P(None, "token"),
            P("token"),
            P(),
            P("token"),
        ),
        out_specs=(P(), P("member", "token", None), P("token", None), P()),
        check_vma=False,
    )
```

profile of v0, /device:TPU:64, one launch (start us, length us, event | category | flops | bytes accessed | tf_op | source)
XLA Modules:
  0.0 912.2 jit_solution(12834779146447870691)
XLA Ops:
  8.9 3.9 copy.95
  13.8 2.3 multiply_reduce_fusion.2
  20.3 3.3 convolution_convert_fusion.8
  25.5 3.8 pad_maximum_fusion.1
  29.3 2.8 collective-permute-start
  33.7 3.9 copy.98
  37.7 2.6 multiply_reduce_fusion.1
  40.9 5.7 pad_maximum_fusion
  46.5 2.2 fusion.223
  58.8 7.5 gather_fusion
  66.3 6.1 select_bitcast_fusion
  72.4 2.3 copy.103
  75.3 85.9 %all-gather.2.cloned.1.call-done = f32[8,100,1024]{2,1,0:T(8,128)} async-done(((f32[2,100,1024]{2,1,0:T(8,128)}), f32[8,100,1024]{2,1,0:T(8,128)}) %all-gather.2.cloned.1.call-update) | async-done | bytes 3276816 | tf_op jit(solution)/shard_map/all_gather | solution.py:157
  161.2 3.2 fusion.195
  167.8 6.7 fusion.57
  174.5 3.5 pad_add_fusion
  179.4 2.2 copy.104
  181.7 63.8 %scatter_fusion = f32[2,100,128]{1,0,2:T(2,128)S(1)} fusion(f32[2,100,128]{1,0,2:T(2,128)S(1)} %broadcast_in_dim.59, s32[1024]{0:T(1024)S(1)} %get-tuple-element.163, f32[1024,2,100]{2,1,0:T(2,128)} %copy.104), kind=kCustom, calls=%fused_computation.1 | custom fusion | flops 204800 | bytes 2461696 | tf_op jit(solution)/shard_map/transpose(jvp(jit(_take)))/scatter-add | solution.py:149
  246.8 3.2 bitcast_convert_fusion
  252.3 95.8 %all-reduce.69.cloned.1.call-done = bf16[1024,1024]{1,0:T(8,128)(2,1)} async-done(((bf16[1024,1024]{1,0:T(8,128)(2,1)}), bf16[1024,1024]{1,0:T(8,128)(2,1)}) %all-reduce.69.cloned.1.call-update) | async-done | bytes 2097168 | tf_op jit(solution)/shard_map/psum | solution.py:197
  348.1 4.1 convert_element_type.189
  353.0 2.6 convolution_convert_fusion.7
  356.9 5.8 fusion.5
  362.8 5.8 convolution_convert_fusion.2
  373.9 3.0 fusion.23
  378.2 4.2 collective-permute-start.3
  383.1 7.9 fusion.17
  391.0 79.1 %psum.21 = f32[]{:T(128)} all-reduce(f32[]{:T(128)S(6)} %div.254), channel_id=1, replica_groups=mesh['member'=4,'token'=64] {'member','token'}, use_global_device_ids=true, to_apply=%region_5.6 | all-reduce | flops 1 | bytes 8 | tf_op jit(solution)/shard_map/psum | solution.py:171
  476.0 3.2 add_convert_fusion
  481.1 2.1 reshape.877
  488.1 113.7 %all-reduce.71.cloned.1.call-done = f32[100,1024]{1,0:T(8,128)} async-done(((f32[100,1024]{1,0:T(8,128)}), f32[100,1024]{1,0:T(8,128)}) %all-reduce.71.cloned.1.call-update) | async-done | bytes 409616 | tf_op jit(solution)/shard_map/psum | solution.py:171
  601.8 300.7 %reduce-scatter.2.cloned.1.call-done = f32[16,1024]{1,0:T(8,128)} async-done(((f32[1024,1024]{1,0:T(8,128)}), f32[16,1024]{1,0:T(8,128)}) %reduce-scatter.2.cloned.1.call-update) | async-done | bytes 65552 | tf_op jit(solution)/shard_map/reduce_scatter | solution.py:198
  (161 shorter events, 52.2 us)
Async XLA Ops:
  7.2 48.1 %copy-start = (bf16[1024,1024]{1,0:T(8,128)(2,1)S(1)}, bf16[1024,1024]{1,0:T(8,128)(2,1)}, u32[]{:S(2)}) copy-start(bf16[1024,1024]{1,0:T(8,128)(2,1)} %param.27) | copy-start | bytes 6291460
  7.2 5.6 copy-start.8
  7.2 5.6 copy-start.7
  7.2 5.6 copy-start.41
  7.2 154.0 %all-gather.2.cloned.1.call-start = ((), (), s32[]{:S(2)}) async-start(), calls=%async_computation.1 | async-start | bytes 4259840 | tf_op jit(solution)/shard_map/all_gather | solution.py:157
  25.5 12.1 %copy-start.42 = (s32[1024]{0:T(1024)S(1)}, s32[1024]{0:T(1024)}, u32[]{:S(2)}) copy-start(s32[1024]{0:T(1024)} %param.33) | copy-start | bytes 12292
  29.3 11.2 %collective-permute-start = (bf16[2,2,128,1024]{2,1,3,0:T(2,128)(2,1)}, bf16[2,2,128,1024]{2,1,3,0:T(2,128)(2,1)}, u32[]{:S(2)}, u32[]{:S(2)}) collective-permute-start(bf16[2,2,128,1024]{2,1,3,0:T(2,128)(2,1)} %pad_maximum_fusion.1), channel_id=1, source_target_pairs={{0,1},{1,2},{2,3},{3,4},{4,5},{5,6},{6,7},{7,8},{8,9},{9,10},{10,1... | collective-permute-start | bytes 3145736 | tf_op jit(solution)/shard_map/ppermute | solution.py:17
  32.1 8.4 collective-permute-start.1
  37.6 3.2 copy-start.13
  37.6 3.2 copy-start.14
  40.3 8.9 copy-start.19
  40.3 8.9 copy-start.39
  40.4 10.6 %copy-start.28 = (pred[128,384]{1,0:T(8,128)(4,1)}, pred[128,384]{1,0:T(8,128)(4,1)S(1)}, u32[]{:S(2)}) copy-start(pred[128,384]{1,0:T(8,128)(4,1)S(1)} %and_and_fusion) | copy-start | bytes 147460
  49.2 4.5 copy-start.12
  57.8 103.4 %copy-start.32 = (f32[1024]{0:T(1024)S(1)}, f32[1024]{0:T(1024)}, u32[]{:S(2)}) copy-start(f32[1024]{0:T(1024)} %param.31) | copy-start | bytes 12292
  57.8 103.4 %copy-start.43 = (f32[100]{0:T(128)S(1)}, f32[100]{0:T(128)}, u32[]{:S(2)}) copy-start(f32[100]{0:T(128)} %param.32) | copy-start | bytes 1204
  74.7 273.4 %all-reduce.69.cloned.1.call-start = ((), (), s32[]{:S(2)}) async-start(), calls=%async_computation.2 | async-start | bytes 4194304 | tf_op jit(solution)/shard_map/psum | solution.py:197
  250.0 351.8 %all-reduce.71.cloned.1.call-start = ((), (), s32[]{:S(2)}) async-start(), calls=%async_computation.4 | async-start | bytes 851968 | tf_op jit(solution)/shard_map/psum | solution.py:171
  252.1 650.4 %reduce-scatter.2.cloned.1.call-start = ((), (), s32[]{:S(2)}) async-start(), calls=%async_computation.3 | async-start | bytes 4259840 | tf_op jit(solution)/shard_map/reduce_scatter | solution.py:198
  352.9 4.0 copy-start.29
  356.9 5.8 copy-start.20
  356.9 5.8 copy-start.40
  362.7 5.8 copy-start.47
  376.9 99.1 %collective-permute-start.2 = (bf16[2,2,128,1024]{2,1,3,0:T(2,128)(2,1)}, bf16[2,2,128,1024]{2,1,3,0:T(2,128)(2,1)}, u32[]{:S(2)}, u32[]{:S(2)}) collective-permute-start(bf16[2,2,128,1024]{2,1,3,0:T(2,128)(2,1)} %get-tuple-element.157), channel_id=1, source_target_pairs={{1,0},{2,1},{3,2},{4,3},{5,4},{6,5},{7,6},{8,7},{9,8},{10,9},{11,1... | collective-permute-start | bytes 3145736 | tf_op jit(solution)/shard_map/ppermute | solution.py:28
  378.2 97.8 %collective-permute-start.3 = (bf16[2,2,128,1024]{2,1,3,0:T(2,128)(2,1)}, bf16[2,2,128,1024]{2,1,3,0:T(2,128)(2,1)}, u32[]{:S(2)}, u32[]{:S(2)}) collective-permute-start(bf16[2,2,128,1024]{2,1,3,0:T(2,128)(2,1)} %get-tuple-element.158), channel_id=1, source_target_pairs={{0,1},{1,2},{2,3},{3,4},{4,5},{5,6},{6,7},{7,8},{8,9},{9,10},{10,1... | collective-permute-start | bytes 3145736 | tf_op jit(solution)/shard_map/ppermute | solution.py:28
  383.0 89.5 %copy-start.38 = (f32[256,16]{0,1:T(8,128)S(1)}, f32[256,16]{0,1:T(8,128)}, u32[]{:S(2)}) copy-start(f32[256,16]{0,1:T(8,128)} %copy-done.37) | copy-start | bytes 49156
  470.7 3.8 copy-start.21
  472.5 3.5 copy-start.6
  479.3 4.0 copy-start.10
  479.3 4.1 copy-start.36
  479.3 4.2 copy-start.31
  485.8 418.5 %copy-start.1 = (bf16[1024,1024]{1,0:T(8,128)(2,1)S(1)}, bf16[1024,1024]{1,0:T(8,128)(2,1)}, u32[]{:S(2)}) copy-start(bf16[1024,1024]{1,0:T(8,128)(2,1)} %param.27) | copy-start | bytes 6291460
  (24 other events, 35.5 us)
Sparse Core Ops, SparseCore 0:
  74.8 86.3 all-gather.1
  250.1 97.9 all-reduce.68
  354.2 247.5 all-reduce.70
  604.7 297.7 reduce-scatter.1
where the time goes:
time: 922 us; the launch traced here: 912 us
  waiting for transfers between devices  596 us (65%)
  other arithmetic  119 us (13%)
  blocking collectives  79.1 us (9%)
  local copies, waits for them, and re-layouts  45.2 us (5%)
  matrix products  44.6 us (5%)
  between operations  17.3 us (2%)
  starting transfers between devices  10.7 us (1%)
    reduce_scatter x1, waiting for transfers between devices, shards(): lax.psum_scatter(summed, 'token', scatter_dimension=0, tiled=True)  301 us
    psum x1, waiting for transfers between devices, shards(): lax.psum((partial_loss, readout_piece_result), ('member', 'token'))  114 us
    psum x1, waiting for transfers between devices, shards(): lax.psum(product.astype(jnp.bfloat16), 'member').astype(jnp.float32)  95.8 us
    all_gather x1, waiting for transfers between devices, shards(): lax.all_gather(realization_prediction, 'member', axis=0, tiled=True)  85.9 us
    psum x1, blocking collectives, shards(): lax.psum((partial_loss, readout_piece_result), ('member', 'token'))  79.1 us
    scatter-add x1, other arithmetic, decode_tokens(): return jnp.take(mapping_array, point_map, axis=2)  63.8 us
    unnamed x99, local copies, waits for them, and re-layouts  18.8 us
  transfers between devices with their start and end apart: 8, of which 4 were waited for; matrix products, arithmetic and copies ran while one was open for 6% of the time, Pallas kernels for 0%

commit v1 on v0

--- a/solution.py
+++ b/solution.py
@@ -154,7 +154,8 @@
     location_places = realization_prediction.shape[2]
     groups = lax.axis_size("member")
     local_shard = lax.axis_index("member")
-    gathered_lines = lax.all_gather(realization_prediction, "member", axis=0, tiled=True)
+    sent = jnp.stack([realization_prediction] * lax.axis_size("member"))
+    gathered_lines = jnp.concatenate(lax.all_to_all(sent, "member", 0, 0), axis=0)
 
     def score_all(whole):
         return unbiased_ranked_score(

time: 922 us -> 890 us (0.965)
  other arithmetic: 119 us -> 86.1 us
    all_gather x1 -> x0, waiting for transfers between devices: 85.9 us -> none  [shards(): lax.all_gather(realization_prediction, 'member', axis=0, tiled=True)]
    all_to_all x0 -> x1, waiting for transfers between devices: none -> 50 us  [shards(): lax.all_to_all(sent, 'member', 0, 0)]
    psum x1, waiting for transfers between devices: 95.8 us -> 128 us  [shards(): lax.psum(product.astype(jnp.bfloat16), 'member').astype(jnp.float32)]
    scatter-add x1, other arithmetic: 63.8 us -> 33.1 us  [decode_tokens(): return jnp.take(mapping_array, point_map, axis=2)]
    unnamed x99 -> x105, local copies, waits for them, and re-layouts: 18.8 us -> 15.5 us
where the time goes in v1:
time: 890 us; the launch traced here: 886 us
  waiting for transfers between devices  599 us (67%)
  other arithmetic  86.1 us (10%)
  blocking collectives  79 us (9%)
  local copies, waits for them, and re-layouts  46.1 us (5%)
  matrix products  39.6 us (4%)
  starting transfers between devices  18.7 us (2%)
  between operations  17.4 us (2%)
    reduce_scatter x1, waiting for transfers between devices, shards(): lax.psum_scatter(summed, 'token', scatter_dimension=0, tiled=True)  301 us
    psum x1, waiting for transfers between devices, shards(): lax.psum(product.astype(jnp.bfloat16), 'member').astype(jnp.float32)  128 us
    psum x1, waiting for transfers between devices, shards(): lax.psum((partial_loss, readout_piece_result), ('member', 'token'))  120 us
    psum x1, blocking collectives, shards(): lax.psum((partial_loss, readout_piece_result), ('member', 'token'))  79 us
    all_to_all x1, waiting for transfers between devices, shards(): lax.all_to_all(sent, 'member', 0, 0)  50 us
    scatter-add x1, other arithmetic, decode_tokens(): return jnp.take(mapping_array, point_map, axis=2)  33.1 us
  transfers between devices with their start and end apart: 8, of which 4 were waited for; matrix products, arithmetic and copies ran while one was open for 6% of the time, Pallas kernels for 0%

profile of v1, /device:TPU:64, one launch (start us, length us, event | category | flops | bytes accessed | tf_op | source)
XLA Modules:
  0.0 885.5 jit_solution(18044666133952023573)
XLA Ops:
  9.4 3.9 copy.70
  14.3 2.3 multiply_reduce_fusion.2
  20.6 3.3 convolution_convert_fusion.8
  23.8 2.0 copy.71
  25.8 3.8 pad_maximum_fusion.1
  29.6 2.7 collective-permute-start
  34.0 4.0 copy.73
  38.6 2.5 multiply_reduce_fusion.1
  41.4 5.8 pad_maximum_fusion
  47.2 2.2 fusion.223
  56.7 7.5 gather_fusion
  64.2 5.3 select_bitcast_fusion
  69.5 2.2 copy.78
  71.7 3.9 stack.5
  75.6 8.1 all-to-all-start
  84.3 50.0 %all-to-all-done = f32[4,2,100,1024]{3,1,2,0:T(2,128)} async-done(((f32[4,2,100,1024]{3,1,2,0:T(2,128)}), f32[4,2,100,1024]{3,1,2,0:T(2,128)}, u32[]{:S(2)}, u32[]{:S(2)}) %all-to-all-start) | async-done | bytes 3276832 | tf_op jit(solution)/shard_map/all_to_all | solution.py:158
  134.2 2.9 copy.79
  141.9 6.7 fusion.57
  148.6 3.5 pad_add_fusion
  155.0 33.1 %scatter_fusion = f32[2,100,128]{1,0,2:T(2,128)S(1)} fusion(f32[2,100,128]{1,0,2:T(2,128)S(1)} %broadcast_in_dim.59, s32[1024]{0:T(1024)} %get-tuple-element.163, f32[1024,2,100]{2,1,0:T(2,128)S(1)} %copy.80), kind=kCustom, calls=%fused_computation.1 | custom fusion | flops 204800 | bytes 2461696 | tf_op jit(solution)/shard_map/transpose(jvp(jit(_take)))/scatter-add | solution.py:149
  188.6 3.4 bitcast_convert_fusion
  193.3 128.0 %all-reduce.69.cloned.1.call-done = bf16[1024,1024]{1,0:T(8,128)(2,1)} async-done(((bf16[1024,1024]{1,0:T(8,128)(2,1)}), bf16[1024,1024]{1,0:T(8,128)(2,1)}) %all-reduce.69.cloned.1.call-update) | async-done | bytes 2097168 | tf_op jit(solution)/shard_map/psum | solution.py:198
  321.3 4.1 convert_element_type.189
  329.2 5.9 fusion.5
  335.2 3.1 convolution_convert_fusion.2
  342.5 2.9 fusion.23
  346.8 4.2 collective-permute-start.3
  351.6 8.0 fusion.17
  359.6 79.0 %psum.21 = f32[]{:T(128)} all-reduce(f32[]{:T(128)S(6)} %div.254), channel_id=1, replica_groups=mesh['member'=4,'token'=64] {'member','token'}, use_global_device_ids=true, to_apply=%region_5.6 | all-reduce | flops 1 | bytes 8 | tf_op jit(solution)/shard_map/psum | solution.py:172
  444.5 3.2 add_convert_fusion
  455.1 119.9 %all-reduce.71.cloned.1.call-done = f32[100,1024]{1,0:T(8,128)} async-done(((f32[100,1024]{1,0:T(8,128)}), f32[100,1024]{1,0:T(8,128)}) %all-reduce.71.cloned.1.call-update) | async-done | bytes 409616 | tf_op jit(solution)/shard_map/psum | solution.py:172
  575.0 300.8 %reduce-scatter.2.cloned.1.call-done = f32[16,1024]{1,0:T(8,128)} async-done(((f32[1024,1024]{1,0:T(8,128)}), f32[16,1024]{1,0:T(8,128)}) %reduce-scatter.2.cloned.1.call-update) | async-done | bytes 65552 | tf_op jit(solution)/shard_map/reduce_scatter | solution.py:199
  (169 shorter events, 49.7 us)
Async XLA Ops:
  7.2 47.5 %copy-start = (bf16[1024,1024]{1,0:T(8,128)(2,1)S(1)}, bf16[1024,1024]{1,0:T(8,128)(2,1)}, u32[]{:S(2)}) copy-start(bf16[1024,1024]{1,0:T(8,128)(2,1)} %param.27) | copy-start | bytes 6291460
  7.2 6.1 copy-start.6
  7.2 6.1 copy-start.4
  7.2 6.1 copy-start.37
  9.4 4.2 copy-start.43
  16.7 9.2 %copy-start.31 = (f32[256,16]{0,1:T(8,128)}, f32[256,16]{0,1:T(8,128)S(1)}, u32[]{:S(2)}) copy-start(f32[256,16]{0,1:T(8,128)S(1)} %get-tuple-element.165) | copy-start | bytes 49156
  25.8 12.1 %copy-start.39 = (s32[1024]{0:T(1024)S(1)}, s32[1024]{0:T(1024)}, u32[]{:S(2)}) copy-start(s32[1024]{0:T(1024)} %param.33) | copy-start | bytes 12292
  29.6 11.7 %collective-permute-start = (bf16[2,2,128,1024]{2,1,3,0:T(2,128)(2,1)}, bf16[2,2,128,1024]{2,1,3,0:T(2,128)(2,1)}, u32[]{:S(2)}, u32[]{:S(2)}) collective-permute-start(bf16[2,2,128,1024]{2,1,3,0:T(2,128)(2,1)} %pad_maximum_fusion.1), channel_id=1, source_target_pairs={{0,1},{1,2},{2,3},{3,4},{4,5},{5,6},{6,7},{7,8},{8,9},{9,10},{10,1... | collective-permute-start | bytes 3145736 | tf_op jit(solution)/shard_map/ppermute | solution.py:17
  32.4 8.9 %collective-permute-start.1 = (bf16[2,2,128,1024]{2,1,3,0:T(2,128)(2,1)}, bf16[2,2,128,1024]{2,1,3,0:T(2,128)(2,1)}, u32[]{:S(2)}, u32[]{:S(2)}) collective-permute-start(bf16[2,2,128,1024]{2,1,3,0:T(2,128)(2,1)} %pad_maximum_fusion.1), channel_id=1, source_target_pairs={{1,0},{2,1},{3,2},{4,3},{5,4},{6,5},{7,6},{8,7},{9,8},{10,9},{11,1... | collective-permute-start | bytes 3145736 | tf_op jit(solution)/shard_map/ppermute | solution.py:20
  38.0 3.4 copy-start.13
  41.1 8.3 copy-start.33
  41.1 8.7 copy-start.19
  41.2 8.7 copy-start.35
  49.9 4.8 copy-start.11
  51.7 3.7 copy-start.10
  75.6 58.6 %all-to-all-start = ((f32[4,2,100,1024]{3,1,2,0:T(2,128)}), f32[4,2,100,1024]{3,1,2,0:T(2,128)}, u32[]{:S(2)}, u32[]{:S(2)}) async-start(f32[4,2,100,1024]{3,1,2,0:T(2,128)} %stack.5), calls=%async_computation | async-start | bytes 6553600 | tf_op jit(solution)/shard_map/all_to_all | solution.py:158
  83.7 53.4 %copy-start.28 = (f32[1024]{0:T(1024)S(1)}, f32[1024]{0:T(1024)}, u32[]{:S(2)}) copy-start(f32[1024]{0:T(1024)} %param.31) | copy-start | bytes 12292
  83.7 53.5 %copy-start.40 = (f32[100]{0:T(128)S(1)}, f32[100]{0:T(128)}, u32[]{:S(2)}) copy-start(f32[100]{0:T(128)} %param.32) | copy-start | bytes 1204
  83.7 237.5 %all-reduce.69.cloned.1.call-start = ((), (), s32[]{:S(2)}) async-start(), calls=%async_computation.2 | async-start | bytes 4194304 | tf_op jit(solution)/shard_map/psum | solution.py:198
  188.1 4.0 copy-start.17
  188.6 137.6 %copy-start.14 = (bf16[2,128,1024]{2,1,0:T(8,128)(2,1)}, bf16[2,128,1024]{2,1,0:T(8,128)(2,1)S(1)}, u32[]{:S(2)}) copy-start(bf16[2,128,1024]{2,1,0:T(8,128)(2,1)S(1)} %convolution_convert_fusion.10) | copy-start | bytes 1572868
  192.0 383.0 %all-reduce.71.cloned.1.call-start = ((), (), s32[]{:S(2)}) async-start(), calls=%async_computation.4 | async-start | bytes 851968 | tf_op jit(solution)/shard_map/psum | solution.py:172
  193.1 682.8 %reduce-scatter.2.cloned.1.call-start = ((), (), s32[]{:S(2)}) async-start(), calls=%async_computation.3 | async-start | bytes 4259840 | tf_op jit(solution)/shard_map/reduce_scatter | solution.py:199
  327.7 7.4 slice-start
  329.2 5.9 slice-start.1
  329.2 5.9 copy-start.20
  329.2 5.9 copy-start.36
  345.5 99.0 %collective-permute-start.2 = (bf16[2,2,128,1024]{2,1,3,0:T(2,128)(2,1)}, bf16[2,2,128,1024]{2,1,3,0:T(2,128)(2,1)}, u32[]{:S(2)}, u32[]{:S(2)}) collective-permute-start(bf16[2,2,128,1024]{2,1,3,0:T(2,128)(2,1)} %get-tuple-element.157), channel_id=1, source_target_pairs={{1,0},{2,1},{3,2},{4,3},{5,4},{6,5},{7,6},{8,7},{9,8},{10,9},{11,1... | collective-permute-start | bytes 3145736 | tf_op jit(solution)/shard_map/ppermute | solution.py:28
  346.8 97.7 %collective-permute-start.3 = (bf16[2,2,128,1024]{2,1,3,0:T(2,128)(2,1)}, bf16[2,2,128,1024]{2,1,3,0:T(2,128)(2,1)}, u32[]{:S(2)}, u32[]{:S(2)}) collective-permute-start(bf16[2,2,128,1024]{2,1,3,0:T(2,128)(2,1)} %get-tuple-element.158), channel_id=1, source_target_pairs={{0,1},{1,2},{2,3},{3,4},{4,5},{5,6},{6,7},{7,8},{8,9},{9,10},{10,1... | collective-permute-start | bytes 3145736 | tf_op jit(solution)/shard_map/ppermute | solution.py:28
  351.6 89.5 %copy-start.34 = (f32[256,16]{0,1:T(8,128)S(1)}, f32[256,16]{0,1:T(8,128)}, u32[]{:S(2)}) copy-start(f32[256,16]{0,1:T(8,128)} %copy-done.33) | copy-start | bytes 49156
  439.3 3.6 copy-start.21
  452.7 424.9 %copy-start.1 = (bf16[1024,1024]{1,0:T(8,128)(2,1)S(1)}, bf16[1024,1024]{1,0:T(8,128)(2,1)}, u32[]{:S(2)}) copy-start(bf16[1024,1024]{1,0:T(8,128)(2,1)} %param.27) | copy-start | bytes 6291460
  (27 other events, 44.4 us)
Sparse Core Ops, SparseCore 0:
  192.1 129.1 all-reduce.68
  327.4 247.6 all-reduce.70
  578.1 297.7 reduce-scatter.1
